TPU v7x, 512 devices: a whole 4x8x8 slice. The times are simulated.
512 devices in a mesh: rows: 64 (over z, y), feat: 8 (over x, core).
Axes of the slice: x: 4, y: 8, z: 8, core: 2. Of those that a mesh axis runs over, the one named last changes fastest.
Arguments:
- node_feats: bfloat16 [65536, 256], P('rows', 'feat'), may hold values from -6 to 6
- band_weights: bfloat16 [65536, 384], P('rows'), may hold values from 0 to 1.5, as said below
- far_weights: bfloat16 [65536, 256], P('rows'), may hold values from 0 to 1.5, as said below
- far_owner: int32 [512, 2], P('rows'), may hold values from 0 to 63, all different within a row; in each aligned block of 8 rows (0 to 7, 8 to 15, ...) at most 2 rows name the same one
- far_local: int32 [512, 2], P('rows'), may hold values from 0 to 7
- w_self: bfloat16 [256, 256], replicated, may hold values from -0.375 to 0.375
- w_neigh: bfloat16 [256, 256], replicated, may hold values from -0.375 to 0.375
- bias: float32 [256], P('feat'), may hold values from -3 to 3
- cotangent: bfloat16 [65536, 256], P('rows', 'feat'), may hold values from -16 to 16
Outputs:
- layer_out: bfloat16 [65536, 256], P('rows', 'feat')
- grad_feats: float32 [65536, 256], P('rows', 'feat')
- grad_self: float32 [256, 256], P('feat')
- grad_neigh: float32 [256, 256], P('feat')
Inputs may be any that keep to these rules, and one draw needn't show every extreme that they name: `far_owner`: among the far entries of the 8 row blocks of one device, no owner is named more than 2 times, and in every draw some owner is named exactly 2 times in some device's blocks; the 2 owners of one row block differ. `band_weights`: each row has a positive weight on the node's own entry of its own block; other entries are zero or positive. `far_weights`: entries are zero or positive.
All inputs are finite; a program needn't handle non-finite values.
Results may differ from a plain program's by a relative error of at most 0.0049.
Values may be sent and summed in bfloat16 or wider, within the bound.
No kernel may reach another device: no remote copies, remote signals or barrier semaphores. Data moves between devices by JAX's collectives and lax.ppermute only.
A program may use at most 64 MiB of HBM per device.

v0:
```python
import jax
import jax.numpy as jnp
from jax import lax
from jax.sharding import PartitionSpec as P


def extended(block, sides, width):
    for axis, dim in sides:
        count = lax.axis_size(axis)
        forward = [(i, i + 1) for i in range(count - 1)]
        backward = [(target, source) for source, target in forward]
        low = lax.ppermute(
            lax.slice_in_dim(block, block.shape[dim] - width, None, axis=dim), axis, forward
        )
        high = lax.ppermute(lax.slice_in_dim(block, 0, width, axis=dim), axis, backward)
        block = jnp.concatenate([low, block, high], axis=dim)
    return block


def from_behind(block, axis, distance):
    devices = range(lax.axis_size(axis))
    route = [(i - distance, i) for i in devices if i - distance in devices]
    return lax.ppermute(block, axis, route)


def on_device(
    node_feats, band_weights, far_weights, far_owner, far_local, w_self, w_neigh, bias, cotangent
):
    rows_dev, col_count = node_feats.shape
    tile_size = band_weights.shape[1] // 3
    blocks = rows_dev // tile_size
    fanout = far_owner.shape[1]
    peer_count = lax.axis_size("rows")
    capacity = max(2, 2 * blocks * fanout // peer_count)
    col_start = lax.axis_index("feat") * col_count
    padded = extended(node_feats, (("rows", 0),), tile_size)
    windows = jnp.concatenate(
        [
            padded[offset * tile_size : offset * tile_size + rows_dev].reshape(
                blocks, tile_size, col_count
            )
            for offset in range(3)
        ],
        axis=1,
    )
    band_tiles = band_weights.reshape(blocks, tile_size, 3 * tile_size)
    band_sum = jnp.einsum("bij,bjc->bic", band_tiles, windows, preferred_element_type=jnp.float32)
    owner_ids = far_owner.reshape(-1)
    local_ids = far_local.reshape(-1)
    entries = owner_ids.shape[0]
    same_owner = owner_ids[:, None] == owner_ids[None, :]
    earlier = jnp.arange(entries)[None, :] < jnp.arange(entries)[:, None]
    slot_rank = jnp.sum(jnp.where(same_owner & earlier, 1, 0), axis=1).astype(jnp.int32)
    slot_ids = owner_ids * capacity + slot_rank
    slot_hit = slot_ids[:, None] == jnp.arange(peer_count * capacity, dtype=jnp.int32)[None, :]
    request = (jnp.sum(jnp.where(slot_hit, local_ids[:, None] + 1, 0), axis=0) - 1).reshape(
        peer_count, capacity
    )
    wanted = lax.all_to_all(request, "rows", split_axis=0, concat_axis=0, tiled=True)
    usable = wanted >= 0
    safe_ids = jnp.maximum(wanted, 0)
    own_blocks = node_feats.reshape(blocks, tile_size, col_count)
    outgoing = jnp.where(
        usable[:, :, None, None], own_blocks[safe_ids], jnp.zeros((), jnp.bfloat16)
    )
    incoming = lax.all_to_all(outgoing, "rows", split_axis=0, concat_axis=0, tiled=True)
    fetched = incoming.reshape(peer_count * capacity, tile_size, col_count)[slot_ids].reshape(
        blocks, fanout * tile_size, col_count
    )
    far_tiles = far_weights.reshape(blocks, tile_size, fanout * tile_size)
    far_sum = jnp.einsum("bij,bjc->bic", far_tiles, fetched, preferred_element_type=jnp.float32)
    degree = jnp.sum(band_weights.astype(jnp.float32), axis=1) + jnp.sum(
        far_weights.astype(jnp.float32), axis=1
    )
    neighbours = ((band_sum + far_sum).reshape(rows_dev, col_count) / degree[:, None]).astype(
        jnp.bfloat16
    )
    rows_self = lax.dynamic_slice_in_dim(w_self, col_start, col_count, 0)
    rows_neigh = lax.dynamic_slice_in_dim(w_neigh, col_start, col_count, 0)
    terms = jnp.dot(node_feats, rows_self, preferred_element_type=jnp.float32) + jnp.dot(
        neighbours, rows_neigh, preferred_element_type=jnp.float32
    )
    preact = lax.psum_scatter(terms, "feat", scatter_dimension=1, tiled=True)
    preact = preact + bias
    layer_out = jax.nn.silu(preact).astype(jnp.bfloat16)
    sigmoid_z = jax.nn.sigmoid(preact)
    grad_pre = (
        cotangent.astype(jnp.float32) * sigmoid_z * (1.0 + preact * (1.0 - sigmoid_z))
    ).astype(jnp.bfloat16)
    full_grad = lax.all_gather(grad_pre, "feat", axis=1, tiled=True)
    grad_scale = float(rows_dev * peer_count) ** (-0.5)
    part_self = jnp.einsum("rc,rf->cf", node_feats, full_grad, preferred_element_type=jnp.float32)
    part_neigh = jnp.einsum("rc,rf->cf", neighbours, full_grad, preferred_element_type=jnp.float32)
    sum_self, sum_neigh = lax.psum((part_self, part_neigh), "rows")
    grad_self = sum_self * grad_scale
    grad_neigh = sum_neigh * grad_scale
    dense_grad = jnp.einsum("rf,cf->rc", full_grad, rows_self, preferred_element_type=jnp.float32)
    grad_agg = jnp.einsum("rf,cf->rc", full_grad, rows_neigh, preferred_element_type=jnp.float32)
    grad_neighbours = (grad_agg / degree[:, None]).astype(jnp.bfloat16)
    grad_blocks = grad_neighbours.reshape(blocks, tile_size, col_count)
    grad_windows = jnp.einsum(
        "bij,bic->bjc", band_tiles, grad_blocks, preferred_element_type=jnp.float32
    )
    grad_padded = jnp.zeros((rows_dev + 2 * tile_size, col_count), jnp.float32)
    for offset in range(3):
        piece = grad_windows[:, offset * tile_size : (offset + 1) * tile_size, :].reshape(
            rows_dev, col_count
        )
        grad_padded = grad_padded + jnp.pad(
            piece, ((offset * tile_size, (2 - offset) * tile_size), (0, 0))
        )
    top_rim = grad_padded[:tile_size]
    bottom_rim = grad_padded[rows_dev + tile_size :]
    from_below = from_behind(top_rim, "rows", -1)
    from_above = from_behind(bottom_rim, "rows", 1)
    grad_fetched = jnp.einsum(
        "bij,bic->bjc", far_tiles, grad_blocks, preferred_element_type=jnp.float32
    )
    returning = jnp.zeros((peer_count * capacity, tile_size, col_count), jnp.float32)
    returning = returning.at[slot_ids].set(grad_fetched.reshape(entries, tile_size, col_count))
    returned = lax.all_to_all(
        returning.reshape(peer_count, capacity, tile_size, col_count).astype(jnp.bfloat16),
        "rows",
        split_axis=0,
        concat_axis=0,
        tiled=True,
    ).astype(jnp.float32)
    target_block = jnp.where(usable, wanted, blocks).reshape(-1)
    owed = jnp.zeros((blocks, tile_size * col_count), jnp.float32)
    owed = owed.at[target_block].add(
        returned.reshape(peer_count * capacity, tile_size * col_count), mode="drop"
    )
    interior = (
        dense_grad
        + grad_padded[tile_size : tile_size + rows_dev]
        + owed.reshape(rows_dev, col_count)
    )
    interior = interior.at[:tile_size].add(from_above)
    grad_feats = interior.at[rows_dev - tile_size :].add(from_below)
    return (layer_out, grad_feats, grad_self, grad_neigh)


def solution(mesh):
    in_specs = (
        P("rows", "feat"),
        P("rows", None),
        P("rows", None),
        P("rows", None),
        P("rows", None),
        P(),
        P(),
        P("feat"),
        P("rows", "feat"),
    )
    out_specs = (P("rows", "feat"), P("rows", "feat"), P("feat", None), P("feat", None))
    return jax.shard_map(
        on_device, mesh=mesh, in_specs=in_specs, out_specs=out_specs, check_vma=False
    )
```

profile of v0, /device:TPU:2, one launch (start us, length us, event | category | flops | bytes accessed | tf_op | source)
XLA Modules:
  0.0 326.7 jit_solution(16754911278057413692)
XLA Ops:
  10.0 16.6 %all-to-all-start = ((s32[64,1,2]{2,1,0:T(1,128)}), s32[64,1,2]{2,1,0:T(1,128)S(1)}, u32[]{:S(2)}, u32[]{:S(2)}) async-start(s32[64,1,2]{2,1,0:T(1,128)} %bitcast.2), calls=%async_computation | async-start | bytes 65536 | tf_op jit(solution)/shard_map/all_to_all | solution.py:59
  27.4 11.1 %all-to-all-done = s32[64,1,2]{2,1,0:T(1,128)S(1)} async-done(((s32[64,1,2]{2,1,0:T(1,128)}), s32[64,1,2]{2,1,0:T(1,128)S(1)}, u32[]{:S(2)}, u32[]{:S(2)}) %all-to-all-start) | async-done | bytes 544 | tf_op jit(solution)/shard_map/all_to_all | solution.py:59
  39.0 1.4 fusion.37
  41.6 1.2 broadcast_select_fusion
  42.8 5.5 %all-to-all-start.1 = ((bf16[64,2,128,32]{2,3,1,0:T(8,128)(2,1)}), bf16[64,2,128,32]{2,3,1,0:T(8,128)(2,1)}, u32[]{:S(2)}, u32[]{:S(2)}) async-start(bf16[64,2,128,32]{2,3,1,0:T(8,128)(2,1)} %broadcast_select_fusion), calls=%async_computation.1 | async-start | bytes 2097152 | tf_op jit(solution)/shard_map/all_to_all | solution.py:66
  48.4 3.3 %collective-permute-start = (bf16[128,32]{0,1:T(8,128)(2,1)S(1)}, bf16[128,32]{0,1:T(8,128)(2,1)S(1)}, u32[]{:S(2)}, u32[]{:S(2)}) collective-permute-start(bf16[128,32]{0,1:T(8,128)(2,1)S(1)} %get-tuple-element.41), channel_id=1, source_target_pairs={{0,8},{8,16},{16,24},{24,32},{32,40},{40,48},{48,56},{56,64},{64,7... | collective-permute-start | bytes 24584 | tf_op jit(solution)/shard_map/ppermute | solution.py:12
  51.7 1.3 collective-permute-start.1
  54.7 13.0 %collective-permute-done = bf16[128,32]{0,1:T(8,128)(2,1)S(1)} collective-permute-done((bf16[128,32]{0,1:T(8,128)(2,1)S(1)}, bf16[128,32]{0,1:T(8,128)(2,1)S(1)}, u32[]{:S(2)}, u32[]{:S(2)}) %collective-permute-start) | collective-permute-done | bytes 8224 | tf_op jit(solution)/shard_map/ppermute | solution.py:12
  67.7 3.3 %collective-permute-done.1 = bf16[128,32]{0,1:T(8,128)(2,1)S(1)} collective-permute-done((bf16[128,32]{0,1:T(8,128)(2,1)S(1)}, bf16[128,32]{0,1:T(8,128)(2,1)S(1)}, u32[]{:S(2)}, u32[]{:S(2)}) %collective-permute-start.1) | collective-permute-done | bytes 8224 | tf_op jit(solution)/shard_map/ppermute | solution.py:15
  71.4 5.6 %all-to-all-done.1 = bf16[64,2,128,32]{2,3,1,0:T(8,128)(2,1)} async-done(((bf16[64,2,128,32]{2,3,1,0:T(8,128)(2,1)}), bf16[64,2,128,32]{2,3,1,0:T(8,128)(2,1)}, u32[]{:S(2)}, u32[]{:S(2)}) %all-to-all-start.1) | async-done | bytes 1048608 | tf_op jit(solution)/shard_map/all_to_all | solution.py:66
  77.0 1.8 gather_fusion.1
  79.2 1.3 convolution_add_fusion
  80.5 28.6 %reduce-scatter.2.cloned.1.call-done = f32[1024,32]{0,1:T(8,128)} async-done(((f32[1024,256]{0,1:T(8,128)}), f32[1024,32]{0,1:T(8,128)}) %reduce-scatter.2.cloned.1.call-update) | async-done | bytes 131088 | tf_op jit(solution)/shard_map/reduce_scatter | solution.py:83
  109.2 1.7 multiply_convert_fusion
  110.8 13.8 %all_gather.3 = bf16[1024,256]{0,1:T(8,128)(2,1)S(1)} all-gather(bf16[1024,32]{0,1:T(8,128)(2,1)S(1)} %get-tuple-element.37), channel_id=1, replica_groups=mesh['rows'=64,'feat'=8] {'feat'}, dimensions={1}, use_global_device_ids=true | all-gather | bytes 589824 | tf_op jit(solution)/shard_map/all_gather | solution.py:90
  128.3 13.3 %all-to-all-start.2 = ((bf16[64,2,128,32]{2,3,1,0:T(8,128)(2,1)}), bf16[64,2,128,32]{2,3,1,0:T(8,128)(2,1)S(1)}, u32[]{:S(2)}, u32[]{:S(2)}) async-start(bf16[64,2,128,32]{2,3,1,0:T(8,128)(2,1)} %bitcast.88), calls=%async_computation.3 | async-start | bytes 2097152 | tf_op jit(solution)/shard_map/all_to_all | solution.py:121
  144.0 3.5 %collective-permute-start.2 = (f32[128,32]{0,1:T(8,128)S(1)}, f32[128,32]{0,1:T(8,128)S(1)}, u32[]{:S(2)}, u32[]{:S(2)}) collective-permute-start(f32[128,32]{0,1:T(8,128)S(1)} %get-tuple-element.33), channel_id=1, source_target_pairs={{0,8},{8,16},{16,24},{24,32},{32,40},{40,48},{48,56},{56,64},{64,7... | collective-permute-start | bytes 49160 | tf_op jit(solution)/shard_map/ppermute | solution.py:23
  147.5 1.5 collective-permute-start.3
  148.9 151.1 %all-reduce.6.cloned.1.call-done = (f32[32,256]{1,0:T(8,128)}, f32[32,256]{1,0:T(8,128)}) async-done(((f32[32,256]{1,0:T(8,128)}, f32[32,256]{1,0:T(8,128)}), (f32[32,256]{1,0:T(8,128)}, f32[32,256]{1,0:T(8,128)})) %all-reduce.6.cloned.1.call-update) | async-done | bytes 65552 | tf_op jit(solution)/shard_map/psum | solution.py:94
  300.0 1.4 broadcast_multiply_fusion.1
  301.4 1.4 broadcast_multiply_fusion
  302.8 4.1 %copy.105 = f32[64,2,128,32]{3,2,1,0:T(8,128)} copy(bf16[64,2,128,32]{2,3,1,0:T(8,128)(2,1)S(1)} %all-to-all-done.2) | data formatting | bytes 3145728 | tf_op jit(solution)/shard_map/reshape | solution.py:131
  306.9 6.2 %reshape.273 = f32[128,4096]{1,0:T(8,128)S(1)} reshape(f32[64,2,128,32]{3,2,1,0:T(8,128)} %copy.105) | data formatting | bytes 4194304 | tf_op jit(solution)/shard_map/reshape | solution.py:131
  313.1 3.8 %scatter_custom_fusion.1 = f32[8,4096]{1,0:T(8,128)} fusion(s32[128]{0:T(128)S(1)} %fusion.32, f32[128,4096]{1,0:T(8,128)S(1)} %reshape.273, f32[]{:T(128)} %constant.91.clone.1), kind=kCustom, calls=%fused_computation.47 | custom fusion | flops 524288 | bytes 131076 | tf_op jit(solution)/shard_map/scatter-add | solution.py:130
  (87 shorter events, 16.5 us)
Async XLA Ops:
  7.2 72.0 %copy-start = (bf16[256,256]{1,0:T(8,128)(2,1)S(1)}, bf16[256,256]{1,0:T(8,128)(2,1)}, u32[]{:S(2)}) copy-start(bf16[256,256]{1,0:T(8,128)(2,1)} %param.19) | copy-start | bytes 393220
  10.0 28.5 %all-to-all-start = ((s32[64,1,2]{2,1,0:T(1,128)}), s32[64,1,2]{2,1,0:T(1,128)S(1)}, u32[]{:S(2)}, u32[]{:S(2)}) async-start(s32[64,1,2]{2,1,0:T(1,128)} %bitcast.2), calls=%async_computation | async-start | bytes 65536 | tf_op jit(solution)/shard_map/all_to_all | solution.py:59
  41.5 6.9 %copy-start.5 = (bf16[1024,32]{0,1:T(8,128)(2,1)S(1)}, bf16[1024,32]{0,1:T(8,128)(2,1)}, u32[]{:S(2)}) copy-start(bf16[1024,32]{0,1:T(8,128)(2,1)} %param.13) | copy-start | bytes 196612
  41.5 11.5 %copy-start.9 = (s32[8,2]{0,1:T(2,128)S(1)}, s32[8,2]{0,1:T(2,128)}, u32[]{:S(2)}) copy-start(s32[8,2]{0,1:T(2,128)} %param.16) | copy-start | bytes 196
  41.6 11.6 %copy-start.2 = (bf16[1024,256]{1,0:T(8,128)(2,1)S(1)}, bf16[1024,256]{1,0:T(8,128)(2,1)}, u32[]{:S(2)}) copy-start(bf16[1024,256]{1,0:T(8,128)(2,1)} %param.15) | copy-start | bytes 1572868
  41.6 11.9 %copy-start.1 = (bf16[1024,384]{1,0:T(8,128)(2,1)S(1)}, bf16[1024,384]{1,0:T(8,128)(2,1)}, u32[]{:S(2)}) copy-start(bf16[1024,384]{1,0:T(8,128)(2,1)} %param.14) | copy-start | bytes 2359300
  42.8 34.2 %all-to-all-start.1 = ((bf16[64,2,128,32]{2,3,1,0:T(8,128)(2,1)}), bf16[64,2,128,32]{2,3,1,0:T(8,128)(2,1)}, u32[]{:S(2)}, u32[]{:S(2)}) async-start(bf16[64,2,128,32]{2,3,1,0:T(8,128)(2,1)} %broadcast_select_fusion), calls=%async_computation.1 | async-start | bytes 2097152 | tf_op jit(solution)/shard_map/all_to_all | solution.py:66
  48.3 60.8 %reduce-scatter.2.cloned.1.call-start = ((), (), s32[]{:S(2)}) async-start(), calls=%async_computation.4 | async-start | bytes 1179648 | tf_op jit(solution)/shard_map/reduce_scatter | solution.py:83
  48.4 19.3 %collective-permute-start = (bf16[128,32]{0,1:T(8,128)(2,1)S(1)}, bf16[128,32]{0,1:T(8,128)(2,1)S(1)}, u32[]{:S(2)}, u32[]{:S(2)}) collective-permute-start(bf16[128,32]{0,1:T(8,128)(2,1)S(1)} %get-tuple-element.41), channel_id=1, source_target_pairs={{0,8},{8,16},{16,24},{24,32},{32,40},{40,48},{48,56},{56,64},{64,7... | collective-permute-start | bytes 24584 | tf_op jit(solution)/shard_map/ppermute | solution.py:12
  51.7 19.3 %collective-permute-start.1 = (bf16[128,32]{0,1:T(8,128)(2,1)S(1)}, bf16[128,32]{0,1:T(8,128)(2,1)S(1)}, u32[]{:S(2)}, u32[]{:S(2)}) collective-permute-start(bf16[128,32]{0,1:T(8,128)(2,1)S(1)} %get-tuple-element.42), channel_id=1, source_target_pairs={{8,0},{16,8},{24,16},{32,24},{40,32},{48,40},{56,48},{64,56},{72,6... | collective-permute-start | bytes 24584 | tf_op jit(solution)/shard_map/ppermute | solution.py:15
  78.9 30.3 %copy-start.8 = (bf16[1024,32]{0,1:T(8,128)(2,1)S(1)}, bf16[1024,32]{0,1:T(8,128)(2,1)}, u32[]{:S(2)}) copy-start(bf16[1024,32]{0,1:T(8,128)(2,1)} %param.21) | copy-start | bytes 196612
  78.9 30.2 %copy-start.10 = (f32[32]{0:T(128)S(1)}, f32[32]{0:T(128)}, u32[]{:S(2)}) copy-start(f32[32]{0:T(128)} %param.20) | copy-start | bytes 388
  124.7 0.8 copy-start.3
  127.1 14.5 %copy-start.7 = (s32[64,2]{1,0:T(8,128)S(1)}, s32[64,2]{1,0:T(8,128)}, u32[]{:S(2)}) copy-start(s32[64,2]{1,0:T(8,128)} %get-tuple-element.28) | copy-start | bytes 1540
  128.3 13.9 %copy-start.4 = (bf16[1024,256]{0,1:T(8,128)(2,1)S(1)}, bf16[1024,256]{0,1:T(8,128)(2,1)}, u32[]{:S(2)}) copy-start(bf16[1024,256]{0,1:T(8,128)(2,1)} %copy-done.3) | copy-start | bytes 1572868
  128.3 174.5 %all-to-all-start.2 = ((bf16[64,2,128,32]{2,3,1,0:T(8,128)(2,1)}), bf16[64,2,128,32]{2,3,1,0:T(8,128)(2,1)S(1)}, u32[]{:S(2)}, u32[]{:S(2)}) async-start(bf16[64,2,128,32]{2,3,1,0:T(8,128)(2,1)} %bitcast.88), calls=%async_computation.3 | async-start | bytes 2097152 | tf_op jit(solution)/shard_map/all_to_all | solution.py:121
  141.6 158.5 %all-reduce.6.cloned.1.call-start = ((), (), s32[]{:S(2)}) async-start(), calls=%async_computation.5 | async-start | bytes 131072 | tf_op jit(solution)/shard_map/psum | solution.py:94
  144.0 175.1 %collective-permute-start.2 = (f32[128,32]{0,1:T(8,128)S(1)}, f32[128,32]{0,1:T(8,128)S(1)}, u32[]{:S(2)}, u32[]{:S(2)}) collective-permute-start(f32[128,32]{0,1:T(8,128)S(1)} %get-tuple-element.33), channel_id=1, source_target_pairs={{0,8},{8,16},{16,24},{24,32},{32,40},{40,48},{48,56},{56,64},{64,7... | collective-permute-start | bytes 49160 | tf_op jit(solution)/shard_map/ppermute | solution.py:23
  147.5 171.7 %collective-permute-start.3 = (f32[128,32]{0,1:T(8,128)S(1)}, f32[128,32]{0,1:T(8,128)S(1)}, u32[]{:S(2)}, u32[]{:S(2)}) collective-permute-start(f32[128,32]{0,1:T(8,128)S(1)} %get-tuple-element.32), channel_id=1, source_target_pairs={{8,0},{16,8},{24,16},{32,24},{40,32},{48,40},{56,48},{64,56},{72,6... | collective-permute-start | bytes 49160 | tf_op jit(solution)/shard_map/ppermute | solution.py:23
  319.2 0.7 copy-start.6
Sparse Core Ops, SparseCore 0:
  80.7 28.4 reduce-scatter.1
  146.3 153.6 all-reduce.5
where the time goes:
time: 328 us; the launch traced here: 327 us
  waiting for transfers between devices  213 us (65%)
  starting transfers between devices  45 us (14%)
  local copies, waits for them, and re-layouts  20.8 us (6%)
  between operations  14.5 us (4%)
  blocking collectives  13.8 us (4%)
  other arithmetic  13.6 us (4%)
  matrix products  6.33 us (2%)
    psum x1, waiting for transfers between devices, on_device(): sum_self, sum_neigh = lax.psum((part_self, part_neigh), 'rows')  151 us
    reduce_scatter x1, waiting for transfers between devices, on_device(): preact = lax.psum_scatter(terms, 'feat', scatter_dimension=1, tiled=True)  28.6 us
    all_to_all x1, starting transfers between devices, on_device(): lax.all_to_all(request, 'rows', split_axis=0, concat_axis=0, tiled=True)  16.6 us
    all_gather x1, blocking collectives, on_device(): full_grad = lax.all_gather(grad_pre, 'feat', axis=1, tiled=True)  13.8 us
    all_to_all x1, starting transfers between devices, on_device(): lax.all_to_all(returning.reshape(peer_count, capacity, tile_size, col_cou...  13.3 us
    ppermute x1, waiting for transfers between devices, extended(): lax.ppermute(lax.slice_in_dim(block, block.shape[dim] - width, None, axis...  13 us
    all_to_all x1, waiting for transfers between devices, on_device(): lax.all_to_all(request, 'rows', split_axis=0, concat_axis=0, tiled=True)  11.1 us
    reshape x2, local copies, waits for them, and re-layouts, on_device(): returned.reshape(peer_count * capacity, tile_size * col_count)  10.3 us
  transfers between devices with their start and end apart: 9, of which 6 were waited for; matrix products, arithmetic and copies ran while one was open for 7% of the time, Pallas kernels for 0%

commit v1 on v0

--- a/solution.py
+++ b/solution.py
@@ -2,6 +2,11 @@
 import jax.numpy as jnp
 from jax import lax
 from jax.sharding import PartitionSpec as P
+
+
+def tiled_gather(x, axis, dim):
+    copies = jnp.concatenate([x] * lax.axis_size(axis), axis=dim)
+    return lax.all_to_all(copies, axis, dim, dim, tiled=True)
 
 
 def extended(block, sides, width):
@@ -87,7 +92,7 @@
     grad_pre = (
         cotangent.astype(jnp.float32) * sigmoid_z * (1.0 + preact * (1.0 - sigmoid_z))
     ).astype(jnp.bfloat16)
-    full_grad = lax.all_gather(grad_pre, "feat", axis=1, tiled=True)
+    full_grad = tiled_gather(grad_pre, "feat", 1)
     grad_scale = float(rows_dev * peer_count) ** (-0.5)
     part_self = jnp.einsum("rc,rf->cf", node_feats, full_grad, preferred_element_type=jnp.float32)
     part_neigh = jnp.einsum("rc,rf->cf", neighbours, full_grad, preferred_element_type=jnp.float32)

time: 328 us -> 329 us (level)
  blocking collectives: 13.8 us -> 0 us
  starting transfers between devices: 45 us -> 52.2 us
  local copies, waits for them, and re-layouts: 20.8 us -> 24.9 us
    all_gather x1 -> x0, blocking collectives: 13.8 us -> none  [on_device(): full_grad = lax.all_gather(grad_pre, 'feat', axis=1, tiled=True)]
    all_to_all x0 -> x1, waiting for transfers between devices: none -> 8.78 us  [tiled_gather(): return lax.all_to_all(copies, axis, dim, dim, tiled=True)]
    all_to_all x0 -> x1, starting transfers between devices: none -> 7.01 us  [tiled_gather(): return lax.all_to_all(copies, axis, dim, dim, tiled=True)]
    psum x1, waiting for transfers between devices: 151 us -> 146 us  [on_device(): sum_self, sum_neigh = lax.psum((part_self, part_neigh), 'rows')]
    unnamed x24 -> x30, local copies, waits for them, and re-layouts: 1.92 us -> 5.48 us
  transfers between devices with their start and end apart: 9 -> 10, of which waited for: 6 -> 7; matrix products, arithmetic and copies ran while one was open for 7% -> 8% of each run, Pallas kernels for 0% -> 0%
where the time goes in v1:
time: 329 us; the launch traced here: 328 us
  waiting for transfers between devices  216 us (66%)
  starting transfers between devices  52.2 us (16%)
  local copies, waits for them, and re-layouts  24.9 us (8%)
  between operations  14.5 us (4%)
  other arithmetic  13.8 us (4%)
  matrix products  6.31 us (2%)
    psum x1, waiting for transfers between devices, on_device(): sum_self, sum_neigh = lax.psum((part_self, part_neigh), 'rows')  146 us
    reduce_scatter x1, waiting for transfers between devices, on_device(): preact = lax.psum_scatter(terms, 'feat', scatter_dimension=1, tiled=True)  28.5 us
    all_to_all x1, starting transfers between devices, on_device(): lax.all_to_all(request, 'rows', split_axis=0, concat_axis=0, tiled=True)  16.6 us
    all_to_all x1, starting transfers between devices, on_device(): lax.all_to_all(returning.reshape(peer_count, capacity, tile_size, col_cou...  13.5 us
    ppermute x1, waiting for transfers between devices, extended(): lax.ppermute(lax.slice_in_dim(block, block.shape[dim] - width, None, axis...  13 us
    all_to_all x1, waiting for transfers between devices, on_device(): lax.all_to_all(request, 'rows', split_axis=0, concat_axis=0, tiled=True)  11.1 us
    reshape x2, local copies, waits for them, and re-layouts, on_device(): returned.reshape(peer_count * capacity, tile_size * col_count)  10.3 us
    all_to_all x1, waiting for transfers between devices, tiled_gather(): return lax.all_to_all(copies, axis, dim, dim, tiled=True)  8.78 us
  transfers between devices with their start and end apart: 10, of which 7 were waited for; matrix products, arithmetic and copies ran while one was open for 8% of the time, Pallas kernels for 0%

profile of v1, /device:TPU:2, one launch (start us, length us, event | category | flops | bytes accessed | tf_op | source)
XLA Modules:
  0.0 328.0 jit_solution(11901654825612508072)
XLA Ops:
  10.0 16.6 %all-to-all-start = ((s32[64,1,2]{2,1,0:T(1,128)}), s32[64,1,2]{2,1,0:T(1,128)S(1)}, u32[]{:S(2)}, u32[]{:S(2)}) async-start(s32[64,1,2]{2,1,0:T(1,128)} %bitcast.2), calls=%async_computation | async-start | bytes 65536 | tf_op jit(solution)/shard_map/all_to_all | solution.py:64
  27.4 11.1 %all-to-all-done = s32[64,1,2]{2,1,0:T(1,128)S(1)} async-done(((s32[64,1,2]{2,1,0:T(1,128)}), s32[64,1,2]{2,1,0:T(1,128)S(1)}, u32[]{:S(2)}, u32[]{:S(2)}) %all-to-all-start) | async-done | bytes 544 | tf_op jit(solution)/shard_map/all_to_all | solution.py:64
  41.0 1.2 broadcast_select_fusion
  42.3 5.5 %all-to-all-start.1 = ((bf16[64,2,128,32]{2,3,1,0:T(8,128)(2,1)}), bf16[64,2,128,32]{2,3,1,0:T(8,128)(2,1)}, u32[]{:S(2)}, u32[]{:S(2)}) async-start(bf16[64,2,128,32]{2,3,1,0:T(8,128)(2,1)} %broadcast_select_fusion), calls=%async_computation.1 | async-start | bytes 2097152 | tf_op jit(solution)/shard_map/all_to_all | solution.py:71
  47.9 3.3 %collective-permute-start = (bf16[128,32]{0,1:T(8,128)(2,1)S(1)}, bf16[128,32]{0,1:T(8,128)(2,1)S(1)}, u32[]{:S(2)}, u32[]{:S(2)}) collective-permute-start(bf16[128,32]{0,1:T(8,128)(2,1)S(1)} %get-tuple-element.41), channel_id=1, source_target_pairs={{0,8},{8,16},{16,24},{24,32},{32,40},{40,48},{48,56},{56,64},{64,7... | collective-permute-start | bytes 24584 | tf_op jit(solution)/shard_map/ppermute | solution.py:17
  51.2 1.3 collective-permute-start.1
  54.2 13.0 %collective-permute-done = bf16[128,32]{0,1:T(8,128)(2,1)S(1)} collective-permute-done((bf16[128,32]{0,1:T(8,128)(2,1)S(1)}, bf16[128,32]{0,1:T(8,128)(2,1)S(1)}, u32[]{:S(2)}, u32[]{:S(2)}) %collective-permute-start) | collective-permute-done | bytes 8224 | tf_op jit(solution)/shard_map/ppermute | solution.py:17
  67.2 3.3 collective-permute-done.1
  70.9 5.6 %all-to-all-done.1 = bf16[64,2,128,32]{2,3,1,0:T(8,128)(2,1)} async-done(((bf16[64,2,128,32]{2,3,1,0:T(8,128)(2,1)}), bf16[64,2,128,32]{2,3,1,0:T(8,128)(2,1)}, u32[]{:S(2)}, u32[]{:S(2)}) %all-to-all-start.1) | async-done | bytes 1048608 | tf_op jit(solution)/shard_map/all_to_all | solution.py:71
  76.4 1.8 gather_fusion.1
  78.7 1.3 convolution_add_fusion
  80.0 28.5 %reduce-scatter.2.cloned.1.call-done = f32[1024,32]{0,1:T(8,128)} async-done(((f32[1024,256]{0,1:T(8,128)}), f32[1024,32]{0,1:T(8,128)}) %reduce-scatter.2.cloned.1.call-update) | async-done | bytes 131088 | tf_op jit(solution)/shard_map/reduce_scatter | solution.py:88
  108.5 1.7 constant_dynamic-update-slice_fusion.7
  114.6 7.0 %all-to-all-start.2 = ((bf16[1024,8,32]{0,2,1:T(8,128)(2,1)}), bf16[1024,8,32]{0,2,1:T(8,128)(2,1)S(1)}, u32[]{:S(2)}, u32[]{:S(2)}) async-start(bf16[1024,8,32]{0,2,1:T(8,128)(2,1)} %bitcast.10), calls=%async_computation.3 | async-start | bytes 1048576 | tf_op jit(solution)/shard_map/all_to_all | solution.py:9
  121.7 8.8 %all-to-all-done.2 = bf16[1024,8,32]{0,2,1:T(8,128)(2,1)S(1)} async-done(((bf16[1024,8,32]{0,2,1:T(8,128)(2,1)}), bf16[1024,8,32]{0,2,1:T(8,128)(2,1)S(1)}, u32[]{:S(2)}, u32[]{:S(2)}) %all-to-all-start.2) | async-done | bytes 524320 | tf_op jit(solution)/shard_map/all_to_all | solution.py:9
  133.9 13.5 %all-to-all-start.3 = ((bf16[64,2,128,32]{2,3,1,0:T(8,128)(2,1)}), bf16[64,2,128,32]{2,3,1,0:T(8,128)(2,1)S(1)}, u32[]{:S(2)}, u32[]{:S(2)}) async-start(bf16[64,2,128,32]{2,3,1,0:T(8,128)(2,1)} %bitcast.110), calls=%async_computation.4 | async-start | bytes 2097152 | tf_op jit(solution)/shard_map/all_to_all | solution.py:126
  150.4 3.5 %collective-permute-start.2 = (f32[128,32]{0,1:T(8,128)S(1)}, f32[128,32]{0,1:T(8,128)S(1)}, u32[]{:S(2)}, u32[]{:S(2)}) collective-permute-start(f32[128,32]{0,1:T(8,128)S(1)} %get-tuple-element.35), channel_id=1, source_target_pairs={{0,8},{8,16},{16,24},{24,32},{32,40},{40,48},{48,56},{56,64},{64,7... | collective-permute-start | bytes 49160 | tf_op jit(solution)/shard_map/ppermute | solution.py:28
  153.9 1.5 collective-permute-start.3
  155.4 146.0 %all-reduce.6.cloned.1.call-done = (f32[32,256]{1,0:T(8,128)}, f32[32,256]{1,0:T(8,128)}) async-done(((f32[32,256]{1,0:T(8,128)}, f32[32,256]{1,0:T(8,128)}), (f32[32,256]{1,0:T(8,128)}, f32[32,256]{1,0:T(8,128)})) %all-reduce.6.cloned.1.call-update) | async-done | bytes 65552 | tf_op jit(solution)/shard_map/psum | solution.py:99
  301.4 1.4 broadcast_multiply_fusion.1
  302.7 1.4 broadcast_multiply_fusion
  304.1 4.1 %copy.108 = f32[64,2,128,32]{3,2,1,0:T(8,128)} copy(bf16[64,2,128,32]{2,3,1,0:T(8,128)(2,1)S(1)} %all-to-all-done.3) | data formatting | bytes 3145728 | tf_op jit(solution)/shard_map/reshape | solution.py:136
  308.2 6.2 %reshape.284 = f32[128,4096]{1,0:T(8,128)S(1)} reshape(f32[64,2,128,32]{3,2,1,0:T(8,128)} %copy.108) | data formatting | bytes 4194304 | tf_op jit(solution)/shard_map/reshape | solution.py:136
  314.4 3.8 %scatter_custom_fusion.1 = f32[8,4096]{1,0:T(8,128)} fusion(s32[128]{0:T(128)S(1)} %fusion.38, f32[128,4096]{1,0:T(8,128)S(1)} %reshape.284, f32[]{:T(128)} %constant.91.clone.1), kind=kCustom, calls=%fused_computation.51 | custom fusion | flops 524288 | bytes 131076 | tf_op jit(solution)/shard_map/scatter-add | solution.py:135
  (96 shorter events, 22.3 us)
Async XLA Ops:
  7.2 71.5 %copy-start = (bf16[256,256]{1,0:T(8,128)(2,1)S(1)}, bf16[256,256]{1,0:T(8,128)(2,1)}, u32[]{:S(2)}) copy-start(bf16[256,256]{1,0:T(8,128)(2,1)} %param.19) | copy-start | bytes 393220
  10.0 28.5 %all-to-all-start = ((s32[64,1,2]{2,1,0:T(1,128)}), s32[64,1,2]{2,1,0:T(1,128)S(1)}, u32[]{:S(2)}, u32[]{:S(2)}) async-start(s32[64,1,2]{2,1,0:T(1,128)} %bitcast.2), calls=%async_computation | async-start | bytes 65536 | tf_op jit(solution)/shard_map/all_to_all | solution.py:64
  41.0 6.9 %copy-start.5 = (bf16[1024,32]{0,1:T(8,128)(2,1)S(1)}, bf16[1024,32]{0,1:T(8,128)(2,1)}, u32[]{:S(2)}) copy-start(bf16[1024,32]{0,1:T(8,128)(2,1)} %param.13) | copy-start | bytes 196612
  41.0 11.5 %copy-start.9 = (s32[8,2]{0,1:T(2,128)S(1)}, s32[8,2]{0,1:T(2,128)}, u32[]{:S(2)}) copy-start(s32[8,2]{0,1:T(2,128)} %param.16) | copy-start | bytes 196
  41.0 11.6 %copy-start.2 = (bf16[1024,256]{1,0:T(8,128)(2,1)S(1)}, bf16[1024,256]{1,0:T(8,128)(2,1)}, u32[]{:S(2)}) copy-start(bf16[1024,256]{1,0:T(8,128)(2,1)} %param.15) | copy-start | bytes 1572868
  41.0 11.8 %copy-start.1 = (bf16[1024,384]{1,0:T(8,128)(2,1)S(1)}, bf16[1024,384]{1,0:T(8,128)(2,1)}, u32[]{:S(2)}) copy-start(bf16[1024,384]{1,0:T(8,128)(2,1)} %param.14) | copy-start | bytes 2359300
  42.3 34.2 %all-to-all-start.1 = ((bf16[64,2,128,32]{2,3,1,0:T(8,128)(2,1)}), bf16[64,2,128,32]{2,3,1,0:T(8,128)(2,1)}, u32[]{:S(2)}, u32[]{:S(2)}) async-start(bf16[64,2,128,32]{2,3,1,0:T(8,128)(2,1)} %broadcast_select_fusion), calls=%async_computation.1 | async-start | bytes 2097152 | tf_op jit(solution)/shard_map/all_to_all | solution.py:71
  47.8 60.8 %reduce-scatter.2.cloned.1.call-start = ((), (), s32[]{:S(2)}) async-start(), calls=%async_computation.5 | async-start | bytes 1179648 | tf_op jit(solution)/shard_map/reduce_scatter | solution.py:88
  47.9 19.3 %collective-permute-start = (bf16[128,32]{0,1:T(8,128)(2,1)S(1)}, bf16[128,32]{0,1:T(8,128)(2,1)S(1)}, u32[]{:S(2)}, u32[]{:S(2)}) collective-permute-start(bf16[128,32]{0,1:T(8,128)(2,1)S(1)} %get-tuple-element.41), channel_id=1, source_target_pairs={{0,8},{8,16},{16,24},{24,32},{32,40},{40,48},{48,56},{56,64},{64,7... | collective-permute-start | bytes 24584 | tf_op jit(solution)/shard_map/ppermute | solution.py:17
  51.2 19.3 %collective-permute-start.1 = (bf16[128,32]{0,1:T(8,128)(2,1)S(1)}, bf16[128,32]{0,1:T(8,128)(2,1)S(1)}, u32[]{:S(2)}, u32[]{:S(2)}) collective-permute-start(bf16[128,32]{0,1:T(8,128)(2,1)S(1)} %get-tuple-element.42), channel_id=1, source_target_pairs={{8,0},{16,8},{24,16},{32,24},{40,32},{48,40},{56,48},{64,56},{72,6... | collective-permute-start | bytes 24584 | tf_op jit(solution)/shard_map/ppermute | solution.py:20
  78.3 30.2 %copy-start.8 = (bf16[1024,32]{0,1:T(8,128)(2,1)S(1)}, bf16[1024,32]{0,1:T(8,128)(2,1)}, u32[]{:S(2)}) copy-start(bf16[1024,32]{0,1:T(8,128)(2,1)} %param.21) | copy-start | bytes 196612
  78.4 30.2 %copy-start.10 = (f32[32]{0:T(128)S(1)}, f32[32]{0:T(128)}, u32[]{:S(2)}) copy-start(f32[32]{0:T(128)} %param.20) | copy-start | bytes 388
  114.6 15.9 %all-to-all-start.2 = ((bf16[1024,8,32]{0,2,1:T(8,128)(2,1)}), bf16[1024,8,32]{0,2,1:T(8,128)(2,1)S(1)}, u32[]{:S(2)}, u32[]{:S(2)}) async-start(bf16[1024,8,32]{0,2,1:T(8,128)(2,1)} %bitcast.10), calls=%async_computation.3 | async-start | bytes 1048576 | tf_op jit(solution)/shard_map/all_to_all | solution.py:9
  130.5 0.8 copy-start.3
  132.7 14.8 %copy-start.6 = (f32[1024,32]{0,1:T(8,128)S(1)}, f32[1024,32]{0,1:T(8,128)}, u32[]{:S(2)}) copy-start(f32[1024,32]{0,1:T(8,128)} %reduce-scatter.2.cloned.1.call-done) | copy-start | bytes 393220
  133.9 14.7 %copy-start.4 = (bf16[1024,8,32]{0,2,1:T(8,128)(2,1)S(1)}, bf16[1024,8,32]{0,2,1:T(8,128)(2,1)}, u32[]{:S(2)}) copy-start(bf16[1024,8,32]{0,2,1:T(8,128)(2,1)} %copy-done.3) | copy-start | bytes 1572868
  133.9 170.2 %all-to-all-start.3 = ((bf16[64,2,128,32]{2,3,1,0:T(8,128)(2,1)}), bf16[64,2,128,32]{2,3,1,0:T(8,128)(2,1)S(1)}, u32[]{:S(2)}, u32[]{:S(2)}) async-start(bf16[64,2,128,32]{2,3,1,0:T(8,128)(2,1)} %bitcast.110), calls=%async_computation.4 | async-start | bytes 2097152 | tf_op jit(solution)/shard_map/all_to_all | solution.py:126
  147.4 153.9 %all-reduce.6.cloned.1.call-start = ((), (), s32[]{:S(2)}) async-start(), calls=%async_computation.6 | async-start | bytes 131072 | tf_op jit(solution)/shard_map/psum | solution.py:99
  150.4 170.0 %collective-permute-start.2 = (f32[128,32]{0,1:T(8,128)S(1)}, f32[128,32]{0,1:T(8,128)S(1)}, u32[]{:S(2)}, u32[]{:S(2)}) collective-permute-start(f32[128,32]{0,1:T(8,128)S(1)} %get-tuple-element.35), channel_id=1, source_target_pairs={{0,8},{8,16},{16,24},{24,32},{32,40},{40,48},{48,56},{56,64},{64,7... | collective-permute-start | bytes 49160 | tf_op jit(solution)/shard_map/ppermute | solution.py:28
  153.9 166.5 %collective-permute-start.3 = (f32[128,32]{0,1:T(8,128)S(1)}, f32[128,32]{0,1:T(8,128)S(1)}, u32[]{:S(2)}, u32[]{:S(2)}) collective-permute-start(f32[128,32]{0,1:T(8,128)S(1)} %get-tuple-element.34), channel_id=1, source_target_pairs={{8,0},{16,8},{24,16},{32,24},{40,32},{48,40},{56,48},{64,56},{72,6... | collective-permute-start | bytes 49160 | tf_op jit(solution)/shard_map/ppermute | solution.py:28
  320.5 0.7 copy-start.7
Sparse Core Ops, SparseCore 0:
  80.1 28.3 reduce-scatter.1
  152.2 149.0 all-reduce.5
